TPU v7x, 128 devices: a whole 4x4x4 slice. The times are simulated.
128 devices in a mesh: ang: 4 (over x), slab: 32 (over z, y, core).
Axes of the slice: x: 4, y: 4, z: 4, core: 2. Of those that a mesh axis runs over, the one named last changes fastest.
Arguments:
- projections: bfloat16 [64, 1024, 2048], P('slab', 'ang'), may hold values from -6 to 6
- dest_plane: int32 [64, 1024], P('slab'), may hold values from 0 to 1023, as said below
- sub_offset: int32 [64, 1024], P('slab'), may hold values from 0 to 7, as said below
- ky_bin: int32 [64, 1024], P('slab'), may hold values from 0 to 7, as said below
Outputs:
- volume_real: float32 [1024, 8, 2048], P('slab', None, 'ang')
- volume_imag: float32 [1024, 8, 2048], P('slab', None, 'ang')
Inputs may be any that keep to these rules, and one draw needn't show every extreme that they name: With f = q for q < 512 and q - 1024 otherwise, and an integer s of 8 to 16 for each projection, e = floor(64 * 1024 f / (1024 * s)) and dest_plane = floor(e / 8) + 512. Among the 2 projections of one slab index at most 128 rows fall on one aligned block of 32 planes; some slab index reaches 128. sub_offset = e mod 8 for the e of dest_plane. With f as for dest_plane and an integer r of 1 to 8 for each projection, ky_bin = floor((f + 512) r / 1024).
All inputs are finite; a program needn't handle non-finite values.
Results may differ from a plain program's by a relative error of at most 0.0085.
Values may be sent and summed in bfloat16 or wider, within the bound.
No kernel may reach another device: no remote copies, remote signals or barrier semaphores. Data moves between devices by JAX's collectives and lax.ppermute only.
A program may use at most 192 MiB of HBM per device.

v0:
```python
import math

import jax
import jax.numpy as jnp
from jax import lax
from jax.sharding import PartitionSpec as P

Z_DEV = 32
KY = 8
REG_ITERS = 2


def padded_2(block, sides, width):
    for axis, dim in sides:
        count = lax.axis_size(axis)
        forward = [(i, i + 1) for i in range(count - 1)]
        backward = [(target, source) for source, target in forward]
        low = lax.ppermute(
            lax.slice_in_dim(block, block.shape[dim] - width, None, axis=dim), axis, forward
        )
        high = lax.ppermute(lax.slice_in_dim(block, 0, width, axis=dim), axis, backward)
        block = jnp.concatenate([low, block, high], axis=dim)
    return block


def trig_tables(length):
    row_index = jnp.arange(length, dtype=jnp.int32)[:, None]
    column = jnp.arange(length, dtype=jnp.int32)[None, :]
    phase_angle = (row_index * column % length).astype(jnp.float32) * (2.0 * math.pi / length)
    return (jnp.cos(phase_angle).astype(jnp.bfloat16), jnp.sin(phase_angle).astype(jnp.bfloat16))


def grid_rows(slots, centre, eighth, ky_index, rows, density):
    buffer = jnp.zeros((slots * KY, rows.shape[1]), jnp.float32)
    for shift in range(-2, 4):
        distance = shift - eighth.astype(jnp.float32) * 0.125
        weight = (jnp.exp(-0.5 * distance * distance) * density).astype(jnp.bfloat16)
        weight = lax.optimization_barrier(weight).astype(jnp.float32)
        index = (centre + (shift + 3)) * KY + ky_index
        buffer = buffer.at[index].add(weight[:, None] * rows)
    return buffer.reshape(slots, KY, rows.shape[1])


def on_device(projections, dest_plane, sub_offset, ky_bin):
    count_ang = lax.axis_size("ang")
    count_slab = lax.axis_size("slab")
    local_count, quarter, full_width = projections.shape
    height = quarter * count_ang
    cosines_w, sines_w = trig_tables(full_width)
    table = jnp.concatenate([cosines_w, sines_w], axis=1)
    transformed = jnp.dot(
        projections.reshape(local_count * quarter, full_width),
        table,
        preferred_element_type=jnp.float32,
    )
    row_spectra = jnp.stack([transformed[:, :full_width], -transformed[:, full_width:]], axis=1)
    row_spectra = row_spectra.astype(jnp.bfloat16).reshape(local_count, quarter, 2, full_width)
    cosines_h, sines_h = trig_tables(height)
    unitary = 1.0 / math.sqrt(height * full_width)
    exchanged = lax.all_to_all(row_spectra, "ang", split_axis=3, concat_axis=1, tiled=True)
    flattened = exchanged.reshape(exchanged.shape[0], height, -1)
    half_cols = exchanged.shape[3]
    cosine_part = jnp.einsum(
        "qh,phx->pqx", cosines_h, flattened, preferred_element_type=jnp.float32
    )
    sine_part = jnp.einsum("qh,phx->pqx", sines_h, flattened, preferred_element_type=jnp.float32)
    real_part = cosine_part[:, :, :half_cols] + sine_part[:, :, half_cols:]
    imag_part = cosine_part[:, :, half_cols:] - sine_part[:, :, :half_cols]
    spectrum = (jnp.concatenate([real_part, imag_part], axis=2) * unitary).astype(jnp.bfloat16)
    spectral_rows = spectrum.reshape(local_count * height, -1)
    total_cols = spectral_rows.shape[1]
    planes_all = dest_plane.reshape(-1)
    eighths_all = sub_offset.reshape(-1)
    ky_all = ky_bin.reshape(-1)
    density = 1.0 / math.sqrt(local_count * count_slab)
    capacity = 2 * local_count * height // count_slab
    owner_slab = planes_all // Z_DEV
    onehot = (owner_slab[:, None] == jnp.arange(count_slab, dtype=jnp.int32)[None, :]).astype(
        jnp.int32
    )
    slot_index = jnp.sum(jnp.cumsum(onehot, axis=0) * onehot, axis=1) - 1
    target = owner_slab * capacity + slot_index
    outgoing = (
        jnp.zeros((count_slab * capacity, total_cols), jnp.bfloat16).at[target].set(spectral_rows)
    )
    labels = jnp.full((count_slab * capacity,), -1, jnp.int32)
    labels = labels.at[target].set(
        ((planes_all - owner_slab * Z_DEV) * 8 + eighths_all) * KY + ky_all
    )
    arrived, arrived_tags = (
        lax.all_to_all(
            outgoing.reshape(count_slab, capacity, total_cols),
            "slab",
            split_axis=0,
            concat_axis=0,
            tiled=True,
        ),
        lax.all_to_all(
            labels.reshape(count_slab, capacity), "slab", split_axis=0, concat_axis=0, tiled=True
        ),
    )
    arrived = arrived.reshape(-1, total_cols)
    arrived_tags = arrived_tags.reshape(-1)
    valid_tag = jnp.maximum(arrived_tags, 0)
    arrived_ky = valid_tag % KY
    arrived_eighth = valid_tag // KY % 8
    arrived_plane = valid_tag // (8 * KY)
    padded = grid_rows(Z_DEV + 6, arrived_plane, arrived_eighth, arrived_ky, arrived, density)
    rim_planes = jnp.concatenate([padded[:3], padded[-3:]], axis=0)
    bordered = padded_2(rim_planes.astype(jnp.bfloat16), (("slab", 0),), 3).astype(rim_planes.dtype)
    gridded = padded[3:-3]
    gridded = gridded.at[:3].add(bordered[:3]).at[-3:].add(bordered[-3:])
    iterate = gridded
    for sweep in range(REG_ITERS):
        bordered_planes = padded_2(iterate.astype(jnp.bfloat16), (("slab", 0),), 1).astype(
            iterate.dtype
        )
        iterate = iterate - 0.25 * (
            iterate - gridded + (2.0 * iterate - bordered_planes[:-2] - bordered_planes[2:])
        )
    half_cols = total_cols // 2
    return (iterate[:, :, :half_cols], iterate[:, :, half_cols:])


def solution(mesh):
    placed = (P("slab", "ang", None), P("slab", None), P("slab", None), P("slab", None))
    return jax.shard_map(
        on_device,
        mesh=mesh,
        in_specs=placed,
        out_specs=(P("slab", None, "ang"), P("slab", None, "ang")),
        check_vma=False,
    )
```

profile of v0, /device:TPU:57, one launch (start us, length us, event | category | flops | bytes accessed | tf_op | source)
XLA Modules:
  0.0 636.2 jit_solution(5098539734234178244)
XLA Ops:
  0.6 0.0 copy-start
  0.6 67.8 %sine_convert_fusion = (bf16[2048,2048]{1,0:T(8,128)(2,1)}, bf16[2048,2048]{1,0:T(8,128)(2,1)}) fusion(), kind=kLoop, calls=%fused_computation.30 | loop fusion | flops 67108864 | bytes 16777216 | tf_op jit(solution)/shard_map/convert_element_type | solution.py:30
  68.4 0.0 copy-done
  68.4 17.8 %fusion.23 = f32[512,4096]{1,0:T(8,128)} fusion(bf16[512,2048]{1,0:T(8,128)(2,1)S(1)} %bitcast.129, bf16[2048,2048]{1,0:T(8,128)(2,1)} %get-tuple-element.54, bf16[2048,2048]{1,0:T(8,128)(2,1)} %get-tuple-element.55), kind=kOutput, calls=%fused_computation.43 | convolution fusion | flops 8623489024 | bytes 27262976 | tf_op jit(solution)/shard_map/dot_general | solution.py:51
  86.2 3.9 slice.229
  90.1 2.7 fusion.31
  92.8 6.1 copy.13
  99.0 3.9 copy.14
  102.8 9.1 %pad_maximum_fusion = bf16[2,256,2,2048]{1,0,2,3:T(2,128)(2,1)} fusion(bf16[2,256,1,2048]{1,0,2,3:T(2,128)(2,1)} %copy.14, bf16[2,256,1,2048]{1,0,2,3:T(2,128)(2,1)} %copy.13), kind=kLoop, calls=%fused_computation.56 | loop fusion | flops 2097152 | bytes 8388608 | tf_op jit(solution)/shard_map/stack | solution.py:56
  111.9 0.0 copy-start.3
  111.9 0.0 copy-start.4
  111.9 5.2 all-to-all-start.1
  117.1 0.0 copy-done.3
  117.1 9.1 %reduce-window.6 = s32[32,16,128]{2,1,0:T(8,128)S(1)} reduce-window(s32[32,16,128]{2,1,0:T(8,128)S(1)} %fusion.52, s32[]{:T(128)} %constant.179.clone.1), window={size=1x1x128 pad=0_0x0_0x127_0}, to_apply=%region_0.1 | reduce-window | flops 8323072 | bytes 524292 | tf_op jit(solution)/shard_map/reduce-window
  126.2 0.1 slice.161
  126.4 0.2 copy.16
  126.6 0.2 reduce-window.9
  126.8 0.0 copy-done.4
  126.8 0.0 copy-done.5
  126.8 0.1 broadcast_add_fusion
  127.0 0.1 fusion.51
  127.1 0.1 compare_select_fusion.6
  127.2 8.6 %scatter_custom_fusion = s32[4096]{0:T(1024)} fusion(s32[2048]{0:T(1024)S(1)} %bitcast.157, s32[2048]{0:T(1024)S(1)} %get-tuple-element.52, s32[]{:T(128)} %constant.177.clone.1), kind=kCustom, calls=%fused_computation.168 | custom fusion | bytes 16388 | tf_op jit(solution)/shard_map/scatter | solution.py:87
  135.8 29.5 %all-to-all-done.1 = bf16[2,256,2,2048]{1,0,2,3:T(2,128)(2,1)} async-done(((bf16[2,256,2,2048]{1,0,2,3:T(2,128)(2,1)}), bf16[2,256,2,2048]{1,0,2,3:T(2,128)(2,1)}, u32[]{:S(2)}, u32[]{:S(2)}) %all-to-all-start.1) | async-done | bytes 4194336 | tf_op jit(solution)/shard_map/all_to_all | solution.py:60
  165.3 9.0 %all-to-all-start = ((s32[32,1,128]{2,1,0:T(1,128)}), s32[32,1,128]{2,1,0:T(1,128)S(1)}, u32[]{:S(2)}, u32[]{:S(2)}) async-start(s32[32,1,128]{2,1,0:T(1,128)} %bitcast.5), calls=%async_computation | async-start | bytes 32768 | tf_op jit(solution)/shard_map/all_to_all | solution.py:98
  174.4 20.1 %copy.15 = bf16[2,256,2,4,512]{4,2,1,3,0:T(2,128)(2,1)} copy(bf16[2,256,2,4,512]{1,0,2,4,3:T(2,128)(2,1)} %bitcast.16) | data formatting | bytes 8388608 | tf_op jit(solution)/shard_map/all_to_all | solution.py:60
  194.4 7.8 %reshape.463 = bf16[2,1024,1024]{2,1,0:T(8,128)(2,1)} reshape(bf16[2,4,256,2,512]{4,3,2,1,0:T(2,128)(2,1)} %bitcast.133) | data formatting | bytes 8388608 | tf_op jit(solution)/shard_map/reshape | solution.py:61
  202.2 23.5 %convolution_bitcast_fusion = f32[2,1024,1024]{2,1,0:T(8,128)} fusion(bf16[2,1024,1024]{2,1,0:T(8,128)(2,1)} %reshape.463), kind=kOutput, calls=%fused_computation.64 | convolution fusion | flops 4310695936 | bytes 12582912 | tf_op jit(solution)/shard_map/qh,phx->pqx/dot_general | solution.py:66
  225.7 0.0 copy-done.2
  225.7 21.4 %convolution_bitcast_fusion.1 = f32[2,1024,1024]{2,1,0:T(8,128)} fusion(bf16[2,1024,1024]{2,1,0:T(8,128)(2,1)S(1)} %copy-done.2), kind=kOutput, calls=%fused_computation.65 | convolution fusion | flops 4310695936 | bytes 12582912 | tf_op jit(solution)/shard_map/qh,phx->pqx/dot_general | solution.py:63
  247.1 11.2 %slice_add_fusion = (f32[2,1024,512]{2,1,0:T(8,128)}, f32[2,1024,512]{2,1,0:T(8,128)}) fusion(f32[2,1024,1024]{2,1,0:T(8,128)} %convolution_bitcast_fusion, f32[2,1024,1024]{2,1,0:T(8,128)} %convolution_bitcast_fusion.1), kind=kLoop, calls=%fused_computation.52 | loop fusion | flops 2097152 | bytes 25165824 | tf_op jit(solution)/shard_map/add | solution.py:67
  258.3 15.8 %scatter_custom_fusion.1 = bf16[4096,1024]{1,0:T(8,128)(2,1)} fusion(s32[2048]{0:T(1024)S(1)} %bitcast.158, f32[2048,512]{1,0:T(8,128)} %bitcast.132, f32[]{:T(128)} %constant.217, f32[2048,512]{1,0:T(8,128)} %bitcast.131, f32[]{:T(128)} %constant.201.clone.1, bf16[]{:T(256)} %constant.194.clone.1), kind=kCustom, calls=%fused_computation.50 | custom fusion | flops 6291456 | bytes 16777226 | tf_op jit(solution)/shard_map/scatter | solution.py:84
  274.1 0.0 all-to-all-done
  274.1 7.4 %all-to-all-start.2 = ((bf16[32,128,1024]{2,1,0:T(8,128)(2,1)}), bf16[32,128,1024]{2,1,0:T(8,128)(2,1)}, u32[]{:S(2)}, u32[]{:S(2)}) async-start(bf16[32,128,1024]{2,1,0:T(8,128)(2,1)} %bitcast.130), calls=%async_computation.2 | async-start | bytes 16777216 | tf_op jit(solution)/shard_map/all_to_all | solution.py:91
  281.7 0.1 compare_select_fusion
  281.8 0.2 compare_select_fusion.1
  282.0 101.9 %all-to-all-done.2 = bf16[32,128,1024]{2,1,0:T(8,128)(2,1)} async-done(((bf16[32,128,1024]{2,1,0:T(8,128)(2,1)}), bf16[32,128,1024]{2,1,0:T(8,128)(2,1)}, u32[]{:S(2)}, u32[]{:S(2)}) %all-to-all-start.2) | async-done | bytes 8388640 | tf_op jit(solution)/shard_map/all_to_all | solution.py:91
  383.8 36.3 %scatter_custom_fusion.2 = f32[304,1024]{1,0:T(8,128)S(1)} fusion(s32[4096]{0:T(1024)S(1)} %bitcast.154, bf16[4096,1024]{1,0:T(8,128)(2,1)} %bitcast.27, f32[4096]{0:T(1024)S(1)} %convert_element_type.107, f32[]{:T(128)} %constant.176.clone.1), kind=kCustom, calls=%fused_computation.20 | custom fusion | flops 12582912 | bytes 9650180 | tf_op jit(solution)/shard_map/scatter-add | solution.py:40
  420.1 36.5 %scatter_custom_fusion.3 = f32[304,1024]{1,0:T(8,128)S(1)} fusion(f32[304,1024]{1,0:T(8,128)S(1)} %scatter_custom_fusion.2, s32[4096]{0:T(1024)S(1)} %bitcast.153, bf16[4096,1024]{1,0:T(8,128)(2,1)} %bitcast.27, f32[4096]{0:T(1024)S(1)} %convert_element_type.118), kind=kCustom, calls=%fused_computation.21 | custom fusion | flops 12582912 | bytes 9650176 | tf_op jit(solution)/shard_map/scatter-add | solution.py:40
  456.6 36.5 %scatter_custom_fusion.4 = f32[304,1024]{1,0:T(8,128)S(1)} fusion(f32[304,1024]{1,0:T(8,128)S(1)} %scatter_custom_fusion.3, s32[4096]{0:T(1024)S(1)} %bitcast.152, bf16[4096,1024]{1,0:T(8,128)(2,1)} %bitcast.27, f32[4096]{0:T(1024)S(1)} %convert_element_type.120), kind=kCustom, calls=%fused_computation.22 | custom fusion | flops 12582912 | bytes 9650176 | tf_op jit(solution)/shard_map/scatter-add | solution.py:40
  493.1 36.7 %scatter_custom_fusion.5 = f32[304,1024]{1,0:T(8,128)S(1)} fusion(f32[304,1024]{1,0:T(8,128)S(1)} %scatter_custom_fusion.4, s32[4096]{0:T(1024)S(1)} %bitcast.151, bf16[4096,1024]{1,0:T(8,128)(2,1)} %bitcast.27, f32[4096]{0:T(1024)S(1)} %convert_element_type.122), kind=kCustom, calls=%fused_computation.23 | custom fusion | flops 12582912 | bytes 9650176 | tf_op jit(solution)/shard_map/scatter-add | solution.py:40
  529.8 36.5 %scatter_custom_fusion.6 = f32[304,1024]{1,0:T(8,128)S(1)} fusion(f32[304,1024]{1,0:T(8,128)S(1)} %scatter_custom_fusion.5, s32[4096]{0:T(1024)S(1)} %bitcast.150, bf16[4096,1024]{1,0:T(8,128)(2,1)} %bitcast.27, f32[4096]{0:T(1024)S(1)} %convert_element_type.124), kind=kCustom, calls=%fused_computation.24 | custom fusion | flops 12582912 | bytes 9650176 | tf_op jit(solution)/shard_map/scatter-add | solution.py:40
  566.3 36.5 %scatter_custom_fusion.7 = f32[304,1024]{1,0:T(8,128)S(1)} fusion(f32[304,1024]{1,0:T(8,128)S(1)} %scatter_custom_fusion.6, s32[4096]{0:T(1024)S(1)} %bitcast.149, bf16[4096,1024]{1,0:T(8,128)(2,1)} %bitcast.27, f32[4096]{0:T(1024)S(1)} %convert_element_type.126), kind=kCustom, calls=%fused_computation.25 | custom fusion | flops 12582912 | bytes 9650176 | tf_op jit(solution)/shard_map/scatter-add | solution.py:40
  602.7 0.1 convert.20
  602.8 5.2 collective-permute-start
  608.0 1.9 collective-permute-start.1
  610.0 0.1 slice_bitcast_fusion
  610.1 0.0 collective-permute-done
  610.1 5.5 collective-permute-done.1
  615.6 0.1 convert_element_type.128
  615.7 1.9 collective-permute-start.2
  617.6 2.4 collective-permute-start.3
  620.0 0.0 collective-permute-done.2
  620.1 4.7 collective-permute-done.3
  624.8 0.1 maximum_convert_fusion
  624.9 0.3 fusion.96
  625.2 1.9 collective-permute-start.4
  627.1 2.4 collective-permute-start.5
  629.5 0.0 collective-permute-done.4
  629.5 4.8 collective-permute-done.5
  634.3 0.1 maximum_convert_fusion.1
  634.4 0.5 fusion.45
  634.9 1.0 fusion.98
  635.9 0.0 copy-done.1
  (24 shorter events, 0.2 us)
Async XLA Ops:
  0.6 67.8 %copy-start = (bf16[2,256,2048]{2,1,0:T(8,128)(2,1)S(1)}, bf16[2,256,2048]{2,1,0:T(8,128)(2,1)}, u32[]{:S(2)}) copy-start(bf16[2,256,2048]{2,1,0:T(8,128)(2,1)} %param.8) | copy-start | bytes 6291460
  111.9 5.2 copy-start.3
  111.9 14.9 %copy-start.4 = (s32[2,1024]{1,0:T(2,128)S(1)}, s32[2,1024]{1,0:T(2,128)}, u32[]{:S(2)}) copy-start(s32[2,1024]{1,0:T(2,128)} %param.11) | copy-start | bytes 24580
  111.9 14.9 %copy-start.5 = (s32[2,1024]{1,0:T(2,128)S(1)}, s32[2,1024]{1,0:T(2,128)}, u32[]{:S(2)}) copy-start(s32[2,1024]{1,0:T(2,128)} %param.10) | copy-start | bytes 24580
  111.9 53.4 %all-to-all-start.1 = ((bf16[2,256,2,2048]{1,0,2,3:T(2,128)(2,1)}), bf16[2,256,2,2048]{1,0,2,3:T(2,128)(2,1)}, u32[]{:S(2)}, u32[]{:S(2)}) async-start(bf16[2,256,2,2048]{1,0,2,3:T(2,128)(2,1)} %pad_maximum_fusion), calls=%async_computation.1 | async-start | bytes 8388608 | tf_op jit(solution)/shard_map/all_to_all | solution.py:60
  165.3 108.8 %all-to-all-start = ((s32[32,1,128]{2,1,0:T(1,128)}), s32[32,1,128]{2,1,0:T(1,128)S(1)}, u32[]{:S(2)}, u32[]{:S(2)}) async-start(s32[32,1,128]{2,1,0:T(1,128)} %bitcast.5), calls=%async_computation | async-start | bytes 32768 | tf_op jit(solution)/shard_map/all_to_all | solution.py:98
  202.2 23.5 %copy-start.2 = (bf16[2,1024,1024]{2,1,0:T(8,128)(2,1)S(1)}, bf16[2,1024,1024]{2,1,0:T(8,128)(2,1)}, u32[]{:S(2)}) copy-start(bf16[2,1024,1024]{2,1,0:T(8,128)(2,1)} %reshape.463) | copy-start | bytes 12582916
  274.1 109.7 %all-to-all-start.2 = ((bf16[32,128,1024]{2,1,0:T(8,128)(2,1)}), bf16[32,128,1024]{2,1,0:T(8,128)(2,1)}, u32[]{:S(2)}, u32[]{:S(2)}) async-start(bf16[32,128,1024]{2,1,0:T(8,128)(2,1)} %bitcast.130), calls=%async_computation.2 | async-start | bytes 16777216 | tf_op jit(solution)/shard_map/all_to_all | solution.py:91
  602.8 7.2 %collective-permute-start = (bf16[3,8,1024]{2,1,0:T(8,128)(2,1)S(1)}, bf16[3,8,1024]{2,1,0:T(8,128)(2,1)S(1)}, u32[]{:S(2)}, u32[]{:S(2)}) collective-permute-start(bf16[3,8,1024]{2,1,0:T(8,128)(2,1)S(1)} %get-tuple-element.34), channel_id=1, source_target_pairs={{0,1},{1,2},{2,3},{3,4},{4,5},{5,6},{6,7},{7,8},{8,9},{9,10},{10,1... | collective-permute-start | bytes 147464 | tf_op jit(solution)/shard_map/ppermute | solution.py:18
  608.0 7.5 %collective-permute-start.1 = (bf16[3,8,1024]{2,1,0:T(8,128)(2,1)S(1)}, bf16[3,8,1024]{2,1,0:T(8,128)(2,1)S(1)}, u32[]{:S(2)}, u32[]{:S(2)}) collective-permute-start(bf16[3,8,1024]{2,1,0:T(8,128)(2,1)S(1)} %get-tuple-element.35), channel_id=1, source_target_pairs={{1,0},{2,1},{3,2},{4,3},{5,4},{6,5},{7,6},{8,7},{9,8},{10,9},{11,1... | collective-permute-start | bytes 147464 | tf_op jit(solution)/shard_map/ppermute | solution.py:21
  615.7 4.3 collective-permute-start.2
  617.6 7.2 %collective-permute-start.3 = (bf16[1,8,1024]{2,1,0:T(8,128)(2,1)S(1)}, bf16[1,8,1024]{2,1,0:T(8,128)(2,1)S(1)}, u32[]{:S(2)}, u32[]{:S(2)}) collective-permute-start(bf16[1,8,1024]{2,1,0:T(8,128)(2,1)S(1)} %get-tuple-element.39), channel_id=1, source_target_pairs={{1,0},{2,1},{3,2},{4,3},{5,4},{6,5},{7,6},{8,7},{9,8},{10,9},{11,1... | collective-permute-start | bytes 49160 | tf_op jit(solution)/shard_map/ppermute | solution.py:21
  625.2 4.3 collective-permute-start.4
  627.1 7.2 %collective-permute-start.5 = (bf16[1,8,1024]{2,1,0:T(8,128)(2,1)S(1)}, bf16[1,8,1024]{2,1,0:T(8,128)(2,1)S(1)}, u32[]{:S(2)}, u32[]{:S(2)}) collective-permute-start(bf16[1,8,1024]{2,1,0:T(8,128)(2,1)S(1)} %get-tuple-element.37), channel_id=1, source_target_pairs={{1,0},{2,1},{3,2},{4,3},{5,4},{6,5},{7,6},{8,7},{9,8},{10,9},{11,1... | collective-permute-start | bytes 49160 | tf_op jit(solution)/shard_map/ppermute | solution.py:21
  634.3 1.6 copy-start.1
where the time goes:
time: 645 us; the launch traced here: 636 us
  other arithmetic  336 us (52%)
  waiting for transfers between devices  146 us (23%)
  matrix products  62.7 us (10%)
  local copies, waits for them, and re-layouts  51.9 us (8%)
  starting transfers between devices  37.4 us (6%)
    scatter-add x6, other arithmetic, grid_rows(): buffer = buffer.at[index].add(weight[:, None] * rows)  219 us
    all_to_all x1, waiting for transfers between devices, on_device(): lax.all_to_all(outgoing.reshape(count_slab, capacity, total_cols), 'slab'...  102 us
    convert_element_type x1, other arithmetic, trig_tables(): jnp.sin(phase_angle).astype(jnp.bfloat16)  67.8 us
    all_to_all x1, waiting for transfers between devices, on_device(): lax.all_to_all(row_spectra, 'ang', split_axis=3, concat_axis=1, tiled=True)  29.5 us
    dot_general x1, matrix products, on_device(): jnp.einsum('qh,phx->pqx', sines_h, flattened, preferred_element_type=jnp....  23.5 us
    dot_general x1, matrix products, on_device(): jnp.einsum('qh,phx->pqx', cosines_h, flattened, preferred_element_type=jn...  21.4 us
    all_to_all x1, local copies, waits for them, and re-layouts, on_device(): lax.all_to_all(row_spectra, 'ang', split_axis=3, concat_axis=1, tiled=True)  20.1 us
    dot_general x1, matrix products, on_device(): jnp.dot(projections.reshape(local_count * quarter, full_width), table, pr...  17.8 us
  transfers between devices with their start and end apart: 9, of which 5 were waited for; matrix products, arithmetic and copies ran while one was open for 19% of the time, Pallas kernels for 0%

commit v1 on v0

v1 whole, which is shorter than its diff:
```python
import math

import jax
import jax.numpy as jnp
from jax import lax
from jax.sharding import PartitionSpec as P

KY = 8
NZ = 1024
REG_ITERS = 2
SPREAD_LOW = 2
SPREAD_HIGH = 3
HALO = SPREAD_LOW + SPREAD_HIGH


def phase_parts(rows, cols, length):
    row_index = jnp.arange(rows, dtype=jnp.int32)[:, None]
    column = cols[None, :]
    phase_angle = (row_index * column % length).astype(jnp.float32) * (2.0 * math.pi / length)
    return jnp.cos(phase_angle), jnp.sin(phase_angle)


def trig_tables(length):
    split = 1 << (int(math.log2(length)) // 2)
    cos_hi, sin_hi = phase_parts(length, jnp.arange(length // split, dtype=jnp.int32) * split, length)
    cos_lo, sin_lo = phase_parts(length, jnp.arange(split, dtype=jnp.int32), length)
    cosine = cos_hi[:, :, None] * cos_lo[:, None, :] - sin_hi[:, :, None] * sin_lo[:, None, :]
    sine = sin_hi[:, :, None] * cos_lo[:, None, :] + cos_hi[:, :, None] * sin_lo[:, None, :]
    return cosine.reshape(length, length), sine.reshape(length, length)


def on_device(projections, dest_plane, sub_offset, ky_bin):
    count_ang = lax.axis_size("ang")
    count_slab = lax.axis_size("slab")
    local_count, quarter, full_width = projections.shape
    height = quarter * count_ang
    cols = full_width // count_ang
    nz = NZ
    z_dev = nz // count_slab

    cosines_w, sines_w = trig_tables(full_width)
    table = jnp.stack(
        [cosines_w.reshape(full_width, count_ang, cols), -sines_w.reshape(full_width, count_ang, cols)],
        axis=2,
    ).astype(jnp.bfloat16)
    transformed = jnp.einsum(
        "rw,wdcx->drcx",
        projections.reshape(local_count * quarter, full_width),
        table,
        preferred_element_type=jnp.float32,
    ).astype(jnp.bfloat16)
    exchanged = lax.all_to_all(transformed, "ang", split_axis=0, concat_axis=0, tiled=True)
    exchanged = exchanged.reshape(count_ang, local_count, quarter, 2, cols)
    real_in = exchanged[:, :, :, 0]
    imag_in = exchanged[:, :, :, 1]
    rhs = jnp.stack(
        [jnp.stack([real_in, imag_in], axis=3), jnp.stack([imag_in, -real_in], axis=3)], axis=0
    )
    cosines_h, sines_h = trig_tables(height)
    lhs = jnp.stack([cosines_h, sines_h], axis=1).astype(jnp.bfloat16)
    lhs = lhs.reshape(height, 2, count_ang, quarter)
    unitary = 1.0 / math.sqrt(height * full_width)
    spectrum = jnp.einsum("qcsh,csphdx->pqdx", lhs, rhs, preferred_element_type=jnp.float32)
    spectrum = (spectrum * unitary).astype(jnp.bfloat16)
    total_cols = 2 * cols
    spectral_rows = spectrum.reshape(local_count * height, total_cols)

    per_proj = 2 * z_dev
    capacity = local_count * per_proj
    edges = jnp.arange(count_slab + 1, dtype=jnp.int32) * z_dev
    start = jnp.sum(
        (dest_plane[:, None, :] < edges[None, :, None]).astype(jnp.int32), axis=2
    )
    counts = start[:, 1:] - start[:, :-1]
    slot = jnp.arange(per_proj, dtype=jnp.int32)
    forder = start[:, :-1, None] + slot[None, None, :]
    valid = slot[None, None, :] < counts[:, :, None]
    row_q = (forder + height // 2) % height
    source = jnp.where(valid, row_q + jnp.arange(local_count, dtype=jnp.int32)[:, None, None] * height, 0)
    source = jnp.transpose(source, (1, 0, 2)).reshape(-1)
    valid = jnp.transpose(valid, (1, 0, 2)).reshape(-1)
    outgoing = jnp.where(valid[:, None], spectral_rows[source], jnp.zeros((), jnp.bfloat16))
    block_of = jnp.repeat(jnp.arange(count_slab, dtype=jnp.int32), capacity)
    flat_plane = dest_plane.reshape(-1)[source]
    flat_eighth = sub_offset.reshape(-1)[source]
    flat_ky = ky_bin.reshape(-1)[source]
    labels = jnp.where(
        valid, ((flat_plane - block_of * z_dev) * 8 + flat_eighth) * KY + flat_ky, -1
    )
    arrived = lax.all_to_all(
        outgoing.reshape(count_slab, capacity, total_cols), "slab", split_axis=0, concat_axis=0, tiled=True
    ).reshape(-1, total_cols)
    arrived_tags = lax.all_to_all(
        labels.reshape(count_slab, capacity), "slab", split_axis=0, concat_axis=0, tiled=True
    ).reshape(-1)

    tag_ok = arrived_tags >= 0
    tag = jnp.maximum(arrived_tags, 0)
    arrived_ky = tag % KY
    arrived_eighth = tag // KY % 8
    arrived_plane = tag // (8 * KY)
    density = 1.0 / math.sqrt(local_count * count_slab)
    slots = z_dev + HALO + 1
    dest_index = jnp.arange(slots * KY, dtype=jnp.int32)[:, None]
    weights = jnp.zeros((slots * KY, arrived.shape[0]), jnp.bfloat16)
    for shift in range(-SPREAD_LOW, SPREAD_HIGH + 1):
        distance = shift - arrived_eighth.astype(jnp.float32) * 0.125
        weight = (jnp.exp(-0.5 * distance * distance) * density).astype(jnp.bfloat16)
        index = (arrived_plane + (shift + SPREAD_HIGH)) * KY + arrived_ky
        hit = (dest_index == index[None, :]) & tag_ok[None, :]
        weights = jnp.where(hit, weight[None, :], weights)
    padded = jnp.dot(weights, arrived, preferred_element_type=jnp.float32)
    padded = padded.reshape(slots, KY, total_cols)

    me = lax.axis_index("slab")
    forward = [(i, i + 1) for i in range(count_slab - 1)]
    backward = [(i + 1, i) for i in range(count_slab - 1)]
    from_lower = lax.ppermute(padded[slots - HALO:], "slab", forward)
    from_upper = lax.ppermute(padded[:HALO], "slab", backward)
    window = padded[1:slots - 1]
    wide = z_dev + 2 * REG_ITERS
    gridded = window.at[:HALO].add(from_lower).at[wide - HALO:].add(from_upper)
    plane_global = me * z_dev + jnp.arange(wide, dtype=jnp.int32) - REG_ITERS
    inside = ((plane_global >= 0) & (plane_global < nz))[:, None, None]
    gridded = jnp.where(inside, gridded, 0.0)
    iterate = gridded
    for sweep in range(REG_ITERS):
        centre = iterate[1:-1]
        target = gridded[sweep + 1:wide - sweep - 1]
        iterate = centre - 0.25 * (
            centre - target + (2.0 * centre - iterate[:-2] - iterate[2:])
        )
        iterate = jnp.where(inside[sweep + 1:wide - sweep - 1], iterate, 0.0)
    return (iterate[:, :, :cols], iterate[:, :, cols:])


def solution(mesh):
    placed = (P("slab", "ang", None), P("slab", None), P("slab", None), P("slab", None))
    return jax.shard_map(
        on_device,
        mesh=mesh,
        in_specs=placed,
        out_specs=(P("slab", None, "ang"), P("slab", None, "ang")),
        check_vma=False,
    )
```

time: 645 us -> 343 us (0.53); the launches traced: 636 us -> 341 us
  other arithmetic: 336 us -> 28 us
  local copies, waits for them, and re-layouts: 51.9 us -> 142 us
  waiting for transfers between devices: 146 us -> 108 us
  matrix products: 62.7 us -> 34.4 us
  starting transfers between devices: 37.4 us -> 27.9 us
    scatter-add x8 -> x2, other arithmetic: 219 us -> 0.06 us  [on_device(): gridded = window.at[:HALO].add(from_lower).at[wide - HALO:].add(from_upper)]
    gather x0 -> x4, local copies, waits for them, and re-layouts: none -> 92.7 us  [the longest x1 23.6 us: on_device(): spectral_rows[source]]
    convert_element_type x14 -> x2, other arithmetic: 68.4 us -> 0.06 us  [on_device(): (jnp.exp(-0.5 * distance * distance) * density).astype(jnp.bfloat16)]
    all_to_all x1, waiting for transfers between devices: 29.5 us -> 0.01 us  [on_device(): lax.all_to_all(transformed, 'ang', split_axis=0, concat_axis=0, tiled=True)]
    dot_general x3, matrix products: 62.7 us -> 34.4 us  [the longest x1 12.7 us: on_device(): jnp.einsum('rw,wdcx->drcx', projections.reshape(local_count * quarter, fu...]
    all_to_all x1 -> x0, local copies, waits for them, and re-layouts: 20.1 us -> none  [on_device(): lax.all_to_all(row_spectra, 'ang', split_axis=3, concat_axis=1, tiled=True)]
    scatter x1 -> x0, other arithmetic: 15.8 us -> none  [on_device(): jnp.zeros((count_slab * capacity, total_cols), jnp.bfloat16).at[target]]
    convert_element_type x0 -> x1, local copies, waits for them, and re-layouts: none -> 11.1 us  [on_device(): spectrum = (spectrum * unitary).astype(jnp.bfloat16)]
  transfers between devices with their start and end apart: 9 -> 5, of which waited for: 5 -> 3; matrix products, arithmetic and copies ran while one was open for 19% -> 48% of each run, Pallas kernels for 0% -> 0%
where the time goes in v1:
time: 343 us; the launch traced here: 341 us
  local copies, waits for them, and re-layouts  142 us (41%)
  waiting for transfers between devices  108 us (31%)
  matrix products  34.4 us (10%)
  other arithmetic  28 us (8%)
  starting transfers between devices  27.9 us (8%)
    all_to_all x1, waiting for transfers between devices, on_device(): lax.all_to_all(outgoing.reshape(count_slab, capacity, total_cols), 'slab'...  102 us
    gather x1, local copies, waits for them, and re-layouts, on_device(): spectral_rows[source]  23.6 us
    gather x1, local copies, waits for them, and re-layouts, on_device(): flat_plane = dest_plane.reshape(-1)[source]  23 us
    gather x1, local copies, waits for them, and re-layouts, on_device(): flat_eighth = sub_offset.reshape(-1)[source]  23 us
    gather x1, local copies, waits for them, and re-layouts, on_device(): flat_ky = ky_bin.reshape(-1)[source]  23 us
    dot_general x1, matrix products, on_device(): jnp.einsum('rw,wdcx->drcx', projections.reshape(local_count * quarter, fu...  12.7 us
    another operation x2, other arithmetic  12 us
    dot_general x1, matrix products, on_device(): padded = jnp.dot(weights, arrived, preferred_element_type=jnp.float32)  11.2 us
  transfers between devices with their start and end apart: 5, of which 3 were waited for; matrix products, arithmetic and copies ran while one was open for 48% of the time, Pallas kernels for 0%

profile of v1, /device:TPU:57, one launch (start us, length us, event | category | flops | bytes accessed | tf_op | source)
XLA Modules:
  0.0 341.2 jit_solution(14935466733160071465)
XLA Ops:
  0.6 0.0 copy-start
  0.7 1.0 fusion.80
  1.7 2.1 fusion.65
  3.8 9.2 %subtract_convert_fusion = (bf16[2048,64,32]{0,2,1:T(8,128)(2,1)S(1)}, bf16[2048,64,32]{0,2,1:T(8,128)(2,1)}) fusion(f32[2048,32]{0,1:T(8,128)S(1)} %get-tuple-element.57, f32[2048,64]{0,1:T(8,128)S(1)} %get-tuple-element.52, f32[2048,32]{0,1:T(8,128)S(1)} %get-tuple-element.58, f32[2048,64]{0,1:T(8,128)S(1)} %get-tuple-element.51), kind=kLoop, calls=%fused_computation.9 | loop fusion | flops 37748736 | bytes 18350080 | tf_op jit(solution)/shard_map/convert.7
  13.0 0.0 copy-done
  13.0 12.7 %convert_bitcast_fusion = bf16[4,512,2,512]{1,3,2,0:T(8,128)(2,1)} fusion(bf16[512,2048,1,1]{1,0,3,2:T(8,128)(2,1)S(1)} %bitcast.162, bf16[2048,4,1,512]{0,3,2,1:T(8,128)(2,1)} %bitcast.170, bf16[2048,4,1,512]{0,3,2,1:T(8,128)(2,1)S(1)} %bitcast.169), kind=kOutput, calls=%fused_computation.42 | convolution fusion | flops 8600420352 | bytes 23068672 | tf_op jit(solution)/shard_map/rw,wdcx->drcx/dot_general | solution.py:46
  25.8 5.2 %all-to-all-start.1 = ((bf16[4,512,2,512]{1,3,2,0:T(8,128)(2,1)}), bf16[4,512,2,512]{1,3,2,0:T(8,128)(2,1)}, u32[]{:S(2)}, u32[]{:S(2)}) async-start(bf16[4,512,2,512]{1,3,2,0:T(8,128)(2,1)} %convert_bitcast_fusion), calls=%async_computation.1 | async-start | bytes 8388608 | tf_op jit(solution)/shard_map/all_to_all | solution.py:52
  31.0 0.0 copy-done.5
  31.0 0.7 fusion.58
  31.7 0.1 iota_compare_fusion.6
  31.8 0.1 lt.151
  31.9 0.1 lt.157
  32.0 0.5 fusion.84
  32.5 0.6 fusion.87
  33.1 2.8 subtract_convert_fusion.1
  35.9 4.0 %copy.34 = bf16[1024,1,4,256]{3,0,2,1:T(8,128)(2,1)} copy(bf16[1024,1,4,256]{0,3,2,1:T(8,128)(2,1)} %bitcast.172) | data formatting | bytes 4194304 | tf_op jit(solution)/shard_map/sub | solution.py:27
  39.9 2.6 copy.35
  42.5 0.1 add_add_fusion
  42.6 0.1 add.420
  42.7 0.1 add.422
  42.7 0.1 add.423
  42.9 0.0 copy-done.6
  42.9 0.1 compare_select_fusion
  43.0 23.0 %gather_fusion = s32[4096]{0:T(1024)S(1)} fusion(s32[2048]{0:T(1024)S(1)} %bitcast.164, s32[4096]{0:T(1024)S(1)} %broadcast_clamp_fusion), kind=kCustom, calls=%fused_computation | custom fusion | bytes 49152 | tf_op jit(solution)/shard_map/gather | solution.py:84
  66.0 0.0 copy-start.7
  66.0 23.0 %gather_fusion.1 = s32[4096]{0:T(1024)S(1)} fusion(s32[2048]{0:T(1024)S(1)} %bitcast.163, s32[4096]{0:T(1024)S(1)} %broadcast_clamp_fusion), kind=kCustom, calls=%fused_computation.1 | custom fusion | bytes 49152 | tf_op jit(solution)/shard_map/gather | solution.py:85
  89.1 0.0 copy-done.7
  89.1 23.0 %gather_fusion.2 = s32[4096]{0:T(1024)S(1)} fusion(s32[2048]{0:T(1024)S(1)} %bitcast.165, s32[4096]{0:T(1024)S(1)} %broadcast_clamp_fusion), kind=kCustom, calls=%fused_computation.2 | custom fusion | bytes 49152 | tf_op jit(solution)/shard_map/gather | solution.py:86
  112.1 0.1 lt.146
  112.2 0.1 lt.147
  112.4 0.1 lt.140
  112.4 0.7 compare_select_fusion.3
  113.1 0.0 all-to-all-done.1
  113.1 8.2 %all-to-all-start = ((s32[32,1,128]{2,1,0:T(1,128)}), s32[32,1,128]{2,1,0:T(1,128)S(1)}, u32[]{:S(2)}, u32[]{:S(2)}) async-start(s32[32,1,128]{2,1,0:T(1,128)} %compare_select_fusion.3), calls=%async_computation | async-start | bytes 32768 | tf_op jit(solution)/shard_map/all_to_all | solution.py:93
  121.3 7.0 %reshape.870 = bf16[4,2,256,2,512]{2,1,4,3,0:T(2,128)(2,1)} reshape(bf16[4,512,2,512]{1,3,2,0:T(8,128)(2,1)} %all-to-all-done.1) | data formatting | bytes 8388608 | tf_op jit(solution)/shard_map/reshape | solution.py:53
  128.2 4.7 %fusion.121 = (bf16[4,2,256,1,512]{2,1,4,3,0:T(2,128)(2,1)S(1)}, bf16[4,2,256,1,512]{2,1,4,3,0:T(2,128)(2,1)S(1)}) fusion(bf16[4,2,256,2,512]{2,1,4,3,0:T(2,128)(2,1)} %reshape.870), kind=kLoop, calls=%fused_computation.200 | loop fusion | bytes 8388608 | tf_op jit(solution)/shard_map/slice | solution.py:55
  132.9 0.3 copy.40
  133.2 1.7 copy_negate_fusion
  134.9 7.0 %stack.23 = bf16[1,4,2,256,2,512]{3,2,5,4,1,0:T(2,128)(2,1)} reshape(bf16[4,512,2,512]{1,3,2,0:T(8,128)(2,1)} %all-to-all-done.1) | data formatting | bytes 8388608 | tf_op jit(solution)/shard_map/stack | solution.py:56
  141.9 3.0 copy.33
  144.9 0.4 maximum_bitcast_fusion
  145.3 1.2 copy-done.3
  146.5 0.6 copy-done.4
  147.1 10.5 %fusion.21 = bf16[2,1024,2,512]{1,3,2,0:T(8,128)(2,1)} fusion(bf16[1024,1,4,256]{3,0,2,1:T(8,128)(2,1)S(1)} %copy-done.4, bf16[1024,1,4,256]{3,0,2,1:T(8,128)(2,1)S(1)} %copy-done.3, bf16[1,4,2,256,2,512]{3,5,1,0,4,2:T(8,128)(2,1)S(1)} %maximum_bitcast_fusion, bf16[1,4,2,256,2,512]{3,5,1,0,4,2:T(8,128)(2,1)S(1)} %copy.33), kind=kOutput, calls=%fused_computation.35 | convolution fusion | flops 8600420352 | bytes 16777216 | tf_op jit(solution)/shard_map/qcsh,csphdx->pqdx/dot_general | solution.py:63
  157.6 11.1 %copy.36 = bf16[2,1024,2,512]{3,2,1,0:T(2,128)(2,1)} copy(bf16[2,1024,2,512]{1,3,2,0:T(8,128)(2,1)} %fusion.21) | data formatting | bytes 8388608 | tf_op jit(solution)/shard_map/convert_element_type | solution.py:64
  168.7 5.4 %copy.45 = bf16[256,8,2,512]{3,1,2,0:T(8,128)(2,1)} copy(bf16[256,8,2,512]{3,2,1,0:T(2,128)(2,1)} %bitcast.168) | data formatting | bytes 8388608
  174.1 23.6 %gather_fusion.3 = bf16[4096,1024]{1,0:T(8,128)(2,1)} fusion(bf16[2048,1024]{1,0:T(8,128)(2,1)} %bitcast.166, s32[4096]{0:T(1024)S(1)} %broadcast_clamp_fusion), kind=kCustom, calls=%fused_computation.3 | custom fusion | bytes 16793600 | tf_op jit(solution)/shard_map/gather | solution.py:82
  197.7 7.2 %broadcast_select_fusion = bf16[32,128,1024]{2,1,0:T(8,128)(2,1)} fusion(bf16[32,128,1024]{2,1,0:T(8,128)(2,1)} %bitcast.167, pred[32,128]{1,0:T(8,128)(4,1)S(1)} %lt.157), kind=kLoop, calls=%fused_computation.16 | loop fusion | flops 4194304 | bytes 16781312 | tf_op jit(solution)/shard_map/jit(_where)/select_n | solution.py:82
  204.9 0.0 all-to-all-done
  204.9 7.4 %all-to-all-start.2 = ((bf16[32,128,1024]{2,1,0:T(8,128)(2,1)}), bf16[32,128,1024]{2,1,0:T(8,128)(2,1)}, u32[]{:S(2)}, u32[]{:S(2)}) async-start(bf16[32,128,1024]{2,1,0:T(8,128)(2,1)} %broadcast_select_fusion), calls=%async_computation.2 | async-start | bytes 16777216 | tf_op jit(solution)/shard_map/all_to_all | solution.py:90
  212.4 0.1 slice.119
  212.4 0.1 slice.118
  212.6 101.5 %all-to-all-done.2 = bf16[32,128,1024]{2,1,0:T(8,128)(2,1)} async-done(((bf16[32,128,1024]{2,1,0:T(8,128)(2,1)}), bf16[32,128,1024]{2,1,0:T(8,128)(2,1)}, u32[]{:S(2)}, u32[]{:S(2)}) %all-to-all-start.2) | async-done | bytes 8388640 | tf_op jit(solution)/shard_map/all_to_all | solution.py:90
  314.2 11.2 %fusion.28 = f32[304,1024]{1,0:T(8,128)S(1)} fusion(bf16[4096,1024]{1,0:T(8,128)(2,1)} %bitcast.29, s32[4096]{0:T(1024)S(1)} %get-tuple-element.49, s32[4096]{0:T(1024)S(1)} %get-tuple-element.48, s32[4096]{0:T(1024)S(1)} %get-tuple-element.47, s32[4096]{0:T(1024)S(1)} %get-tuple-element.46, s32[4096]{0:T(1024)S(1)} %get-tuple-element.50, ...), kind=kOutput, calls=%fused_computation.43 | convolution fusion | flops 2572550144 | bytes 9785344 | tf_op jit(solution)/shard_map/dot_general | solution.py:112
  325.4 5.2 %collective-permute-start = (f32[5,8,1024]{2,1,0:T(8,128)S(1)}, f32[5,8,1024]{2,1,0:T(8,128)S(1)}, u32[]{:S(2)}, u32[]{:S(2)}) collective-permute-start(f32[5,8,1024]{2,1,0:T(8,128)S(1)} %get-tuple-element.33), channel_id=1, source_target_pairs={{0,1},{1,2},{2,3},{3,4},{4,5},{5,6},{6,7},{7,8},{8,9},{9,10},{10,1... | collective-permute-start | bytes 491528 | tf_op jit(solution)/shard_map/ppermute | solution.py:118
  330.6 1.9 collective-permute-start.1
  332.5 0.1 slice_bitcast_fusion
  332.6 0.2 collective-permute-done
  332.9 6.5 %collective-permute-done.1 = f32[5,8,1024]{2,1,0:T(8,128)S(1)} collective-permute-done((f32[5,8,1024]{2,1,0:T(8,128)S(1)}, f32[5,8,1024]{2,1,0:T(8,128)S(1)}, u32[]{:S(2)}, u32[]{:S(2)}) %collective-permute-start.1) | collective-permute-done | bytes 163872 | tf_op jit(solution)/shard_map/ppermute | solution.py:119
  339.4 0.1 broadcast_select_fusion.1
  339.5 0.0 copy-start.1
  339.5 0.3 fusion.47
  339.9 0.3 fusion.51
  340.2 1.0 fusion.122
  (25 shorter events, 0.2 us)
Async XLA Ops:
  0.6 12.4 %copy-start = (bf16[2,256,2048]{2,1,0:T(8,128)(2,1)S(1)}, bf16[2,256,2048]{2,1,0:T(8,128)(2,1)}, u32[]{:S(2)}) copy-start(bf16[2,256,2048]{2,1,0:T(8,128)(2,1)} %param.8) | copy-start | bytes 6291460
  25.8 5.2 %copy-start.5 = (s32[2,1024]{1,0:T(2,128)S(1)}, s32[2,1024]{1,0:T(2,128)}, u32[]{:S(2)}) copy-start(s32[2,1024]{1,0:T(2,128)} %param.9) | copy-start | bytes 24580
  25.8 87.3 %all-to-all-start.1 = ((bf16[4,512,2,512]{1,3,2,0:T(8,128)(2,1)}), bf16[4,512,2,512]{1,3,2,0:T(8,128)(2,1)}, u32[]{:S(2)}, u32[]{:S(2)}) async-start(bf16[4,512,2,512]{1,3,2,0:T(8,128)(2,1)} %convert_bitcast_fusion), calls=%async_computation.1 | async-start | bytes 8388608 | tf_op jit(solution)/shard_map/all_to_all | solution.py:52
  35.9 7.0 %copy-start.6 = (s32[2,1024]{1,0:T(2,128)S(1)}, s32[2,1024]{1,0:T(2,128)}, u32[]{:S(2)}) copy-start(s32[2,1024]{1,0:T(2,128)} %param.10) | copy-start | bytes 24580
  66.0 23.1 %copy-start.7 = (s32[2,1024]{1,0:T(2,128)S(1)}, s32[2,1024]{1,0:T(2,128)}, u32[]{:S(2)}) copy-start(s32[2,1024]{1,0:T(2,128)} %param.11) | copy-start | bytes 24580
  113.1 91.8 %all-to-all-start = ((s32[32,1,128]{2,1,0:T(1,128)}), s32[32,1,128]{2,1,0:T(1,128)S(1)}, u32[]{:S(2)}, u32[]{:S(2)}) async-start(s32[32,1,128]{2,1,0:T(1,128)} %compare_select_fusion.3), calls=%async_computation | async-start | bytes 32768 | tf_op jit(solution)/shard_map/all_to_all | solution.py:93
  141.9 3.0 copy-start.2
  144.9 1.6 copy-start.3
  144.9 2.2 copy-start.4
  204.9 109.3 %all-to-all-start.2 = ((bf16[32,128,1024]{2,1,0:T(8,128)(2,1)}), bf16[32,128,1024]{2,1,0:T(8,128)(2,1)}, u32[]{:S(2)}, u32[]{:S(2)}) async-start(bf16[32,128,1024]{2,1,0:T(8,128)(2,1)} %broadcast_select_fusion), calls=%async_computation.2 | async-start | bytes 16777216 | tf_op jit(solution)/shard_map/all_to_all | solution.py:90
  325.4 7.4 %collective-permute-start = (f32[5,8,1024]{2,1,0:T(8,128)S(1)}, f32[5,8,1024]{2,1,0:T(8,128)S(1)}, u32[]{:S(2)}, u32[]{:S(2)}) collective-permute-start(f32[5,8,1024]{2,1,0:T(8,128)S(1)} %get-tuple-element.33), channel_id=1, source_target_pairs={{0,1},{1,2},{2,3},{3,4},{4,5},{5,6},{6,7},{7,8},{8,9},{9,10},{10,1... | collective-permute-start | bytes 491528 | tf_op jit(solution)/shard_map/ppermute | solution.py:118
  330.6 8.7 %collective-permute-start.1 = (f32[5,8,1024]{2,1,0:T(8,128)S(1)}, f32[5,8,1024]{2,1,0:T(8,128)S(1)}, u32[]{:S(2)}, u32[]{:S(2)}) collective-permute-start(f32[5,8,1024]{2,1,0:T(8,128)S(1)} %get-tuple-element.32), channel_id=1, source_target_pairs={{1,0},{2,1},{3,2},{4,3},{5,4},{6,5},{7,6},{8,7},{9,8},{10,9},{11,1... | collective-permute-start | bytes 491528 | tf_op jit(solution)/shard_map/ppermute | solution.py:119
  339.5 1.7 copy-start.1
